TPU v7x, 512 devices: a whole 4x4x16 slice. The times are simulated.
512 devices in a mesh: dp: 4 (over z_hi, core), tm: 8 (over z_lo), height: 16 (over x, y).
Axes of the slice: x: 4, y: 4, z: 16 (z_hi: 2, z_lo: 8; z = z_hi * 8 + z_lo), core: 2. Of those that a mesh axis runs over, the one named last changes fastest.
Arguments:
- clips: bfloat16 [4, 16, 64, 128, 128], P('dp', 'tm', 'height'), may hold values from -6 to 6
- frame_counts: int32 [4, 5], P('dp'), may hold values from 1 to 9, 16 in all within a row
- conv_first: bfloat16 [3, 3, 3, 128, 128], replicated, may hold values from -0.109375 to 0.109375
- conv_down: bfloat16 [3, 3, 3, 128, 128], replicated, may hold values from -0.109375 to 0.109375
- out_cotangent: bfloat16 [4, 8, 32, 64, 128], P('dp', 'tm', 'height'), may hold values from -6 to 6
Outputs:
- encoded: bfloat16 [4, 8, 32, 64, 128], P('dp', 'tm', 'height')
- grad_first: bfloat16 [3, 3, 3, 128, 128], P(None, None, None, 'dp')
- grad_down: bfloat16 [3, 3, 3, 128, 128], P(None, None, None, 'dp')
Inputs may be any that keep to these rules, and one draw needn't show every extreme that they name: `frame_counts`: each sequence's 5 clip lengths sum to 16; in every sequence one clip has exactly 9 frames.
All inputs are finite; a program needn't handle non-finite values.
Results may differ from a plain program's by a relative error of at most 0.0059.
Values may be sent and summed in bfloat16 or wider, within the bound.
No kernel may reach another device: no remote copies, remote signals or barrier semaphores. Data moves between devices by JAX's collectives and lax.ppermute only.
A program may use at most 64 MiB of HBM per device.

v0:
```python
import math
import jax
import jax.numpy as jnp
from jax import lax
from jax.sharding import PartitionSpec as P


def padded_2(cells, sides, width):
    for axis, dim in sides:
        count = lax.axis_size(axis)
        ends = count - 1
        head = lax.slice_in_dim(cells, 0, width, axis=dim)
        tail = lax.slice_in_dim(cells, cells.shape[dim] - width, cells.shape[dim], axis=dim)
        cells = jnp.concatenate(
            [
                lax.ppermute(tail, axis, [(i, (i + 1) % count) for i in range(ends)]),
                cells,
                lax.ppermute(head, axis, [((i + 1) % count, i) for i in range(ends)]),
            ],
            axis=dim,
        )
    return cells


def shifted(value, axis, steps):
    count = lax.axis_size(axis)
    leading, last = (max(0, -steps), min(count, count - steps))
    return lax.ppermute(value, axis, [(source, source + steps) for source in range(leading, last)])


def unfold(frame_slab, stride, pad_cols):
    padded = jnp.pad(frame_slab, ((0, 0), (0, 0), pad_cols, (0, 0)))
    out_rows = (padded.shape[1] - 3) // stride + 1
    out_cols = (padded.shape[2] - 3) // stride + 1
    pieces = []
    for tap_row in range(3):
        for tap_col in range(3):
            pieces.append(
                padded[
                    :,
                    tap_row : tap_row + stride * (out_rows - 1) + 1 : stride,
                    tap_col : tap_col + stride * (out_cols - 1) + 1 : stride,
                ]
            )
    joined = jnp.concatenate(pieces, axis=-1)
    return (joined.reshape(-1, joined.shape[-1]), (frame_slab.shape[0], out_rows, out_cols))


def conv_layer(extended, weight, tap_mask, out_frames, stride, pad_cols):
    channels_out = weight.shape[-1]
    summed = None
    for tap_time in range(3):
        frame_slab = extended[tap_time : tap_time + stride * (out_frames - 1) + 1 : stride]
        columns, shape_out = unfold(frame_slab, stride, pad_cols)
        kernel = weight[tap_time].reshape(-1, channels_out)
        tap_term = jnp.dot(columns, kernel, preferred_element_type=jnp.float32).reshape(
            shape_out + (channels_out,)
        )
        tap_term = tap_term * tap_mask[:, tap_time][:, None, None, None]
        summed = tap_term if summed is None else summed + tap_term
    return summed


def weight_grad(extended, grads, tap_mask, stride, pad_cols):
    out_frames = grads.shape[0]
    blocks = []
    for tap_time in range(3):
        frame_slab = extended[tap_time : tap_time + stride * (out_frames - 1) + 1 : stride]
        columns, shape_out = unfold(frame_slab, stride, pad_cols)
        masked = grads * tap_mask[:, tap_time].astype(jnp.bfloat16)[:, None, None, None]
        blocks.append(
            jnp.dot(
                columns.T, masked.reshape(-1, grads.shape[-1]), preferred_element_type=jnp.float32
            )
        )
    stacked = jnp.stack(blocks)
    return stacked.reshape(3, 3, 3, extended.shape[-1], grads.shape[-1])


def hidden_grad(grads_ext, weight, mask_ext):
    pieces = []
    for tap_time in range(3):
        masked = grads_ext * mask_ext[:, tap_time].astype(jnp.bfloat16)[:, None, None, None]
        kernel = jnp.transpose(weight[tap_time][::-1, ::-1], (0, 1, 3, 2))
        spread = lax.conv_general_dilated(
            masked,
            kernel,
            (1, 1),
            ((2, 0), (2, 2)),
            lhs_dilation=(2, 2),
            dimension_numbers=("NHWC", "HWIO", "NHWC"),
            preferred_element_type=jnp.float32,
        )
        pieces.append(spread[:, 1:, 1:])
    even_frames = pieces[2][:-1] + pieces[0][1:]
    odd_frames = pieces[1][1:]
    merged = jnp.stack([even_frames, odd_frames], axis=1)
    return merged.reshape((2 * even_frames.shape[0],) + even_frames.shape[1:])


def positions(counts_row, frame_index):
    starts = jnp.cumsum(counts_row) - counts_row
    latest = jnp.max(jnp.where(starts[None, :] <= frame_index[:, None], starts[None, :], 0), axis=1)
    return frame_index - latest


def tap_masks(place):
    return (place[:, None] >= (2 - jnp.arange(3, dtype=jnp.int32))[None, :]).astype(jnp.float32)


def body(clips, frame_counts, conv_first, conv_down, out_cotangent):
    frames_dev = clips.shape[1]
    rows_dev = clips.shape[2]
    columns_all = clips.shape[3]
    down_frames = frames_dev // 2
    counts_row = frame_counts[0]
    first_frame = lax.axis_index("tm") * frames_dev
    frame_index = first_frame + jnp.arange(frames_dev, dtype=jnp.int32)
    first_mask = tap_masks(positions(counts_row, frame_index))
    down_index = first_frame + 2 * jnp.arange(down_frames + 1, dtype=jnp.int32)
    mask_ext = tap_masks(positions(counts_row, down_index))
    down_mask = mask_ext[:down_frames]
    with_rows = padded_2(clips[0], (("height", 1),), 1)
    earlier = shifted(with_rows, "tm", 1)
    input_ext = jnp.concatenate([earlier, with_rows], axis=0)
    pre_act = conv_layer(input_ext, conv_first, first_mask, frames_dev, 1, (1, 1))
    hidden = jax.nn.silu(pre_act).astype(jnp.bfloat16)
    above = shifted(hidden[:, rows_dev - 1 :], "height", 1)
    hidden_rows = jnp.concatenate([above, hidden], axis=1)
    hidden_past = shifted(hidden_rows, "tm", 1)
    hidden_ext = jnp.concatenate([hidden_past, hidden_rows], axis=0)
    encoded = conv_layer(hidden_ext, conv_down, down_mask, down_frames, 2, (1, 0)).astype(
        jnp.bfloat16
    )
    cells_all = (
        lax.axis_size("dp")
        * clips.shape[0]
        * down_frames
        * lax.axis_size("tm")
        * (rows_dev // 2)
        * lax.axis_size("height")
        * (columns_all // 2)
    )
    scale = 1.0 / math.sqrt(cells_all)
    grads = (out_cotangent[0].astype(jnp.float32) * scale).astype(jnp.bfloat16)
    down_local = weight_grad(hidden_ext, grads, down_mask, 2, (1, 0))
    below = shifted(grads[:, 0:1], "height", -1)
    grads_rows = jnp.concatenate([grads, below], axis=1)
    grads_next = shifted(grads_rows, "tm", -1)
    grads_ext = jnp.concatenate([grads_rows, grads_next], axis=0)
    back_hidden = hidden_grad(grads_ext, conv_down, mask_ext).astype(jnp.bfloat16)
    sigma = jax.nn.sigmoid(pre_act)
    pre_grad = (back_hidden.astype(jnp.float32) * sigma * (1.0 + pre_act * (1.0 - sigma))).astype(
        jnp.bfloat16
    )
    first_local = weight_grad(input_ext, pre_grad, first_mask, 1, (1, 1))
    share = conv_first.shape[3] // lax.axis_size("dp")
    quarters = lax.axis_size("dp")

    def by_quarter(term):
        term = term.reshape(27, quarters, share, term.shape[-1])
        return jnp.transpose(term, (1, 0, 2, 3)).reshape(quarters, -1)

    stacked = jnp.concatenate([by_quarter(first_local), by_quarter(down_local)], axis=1)
    rows_n, frames_n = (lax.axis_size("height"), lax.axis_size("tm"))
    piece = stacked.reshape(quarters, rows_n, frames_n, -1)
    piece = lax.psum_scatter(piece, "height", scatter_dimension=1, tiled=True)
    piece = lax.psum_scatter(piece, "tm", scatter_dimension=2, tiled=True)
    piece = lax.psum_scatter(piece, "dp", scatter_dimension=0, tiled=True)
    piece = piece.astype(jnp.bfloat16)
    piece = lax.all_gather(piece, "tm", axis=2, tiled=True)
    gathered = lax.all_gather(piece, "height", axis=1, tiled=True).reshape(-1)
    half = gathered.shape[0] // 2
    kernel_shape = (3, 3, 3, share, conv_first.shape[-1])
    summed_first = gathered[:half].reshape(kernel_shape)
    summed_down = gathered[half:].reshape(kernel_shape)
    return (encoded[None], summed_first, summed_down)


def solution(mesh):
    in_specs = (
        P("dp", "tm", "height", None, None),
        P("dp", None),
        P(),
        P(),
        P("dp", "tm", "height", None, None),
    )
    out_specs = (
        P("dp", "tm", "height", None, None),
        P(None, None, None, "dp", None),
        P(None, None, None, "dp", None),
    )
    return jax.shard_map(body, mesh=mesh, in_specs=in_specs, out_specs=out_specs, check_vma=False)
```

profile of v0, /device:TPU:32, one launch (start us, length us, event | category | flops | bytes accessed | tf_op | source)
XLA Modules:
  0.0 460.8 jit_solution(5492218654866860973)
XLA Ops:
  7.2 0.9 fusion.92
  8.1 3.5 collective-permute-start
  11.6 1.3 collective-permute-start.1
  12.9 0.8 fusion.60
  13.7 1.3 collective-permute-start.5
  15.0 0.8 reduce-window_clone.1
  16.9 1.2 fusion.89
  21.7 5.2 %collective-permute-start.6 = (bf16[1,3,64,128]{3,2,1,0:T(8,128)(2,1)S(1)}, bf16[1,3,64,128]{3,2,1,0:T(8,128)(2,1)S(1)}, u32[]{:S(2)}, u32[]{:S(2)}) collective-permute-start(bf16[1,3,64,128]{3,2,1,0:T(8,128)(2,1)S(1)} %pad_maximum_fusion.8), channel_id=1, source_target_pairs={{16,0},{32,16},{48,32},{64,48},{80,64},{96,80},{112,96},{17,1},{33... | collective-permute-start | bytes 147464 | tf_op jit(solution)/shard_map/ppermute | solution.py:28
  27.0 2.1 collective-permute-start.2
  29.2 1.3 multiply_bitcast_fusion.1
  33.1 3.8 collective-permute-done.2
  37.9 0.8 convolution_multiply_fusion.1
  39.6 0.8 fusion.1
  40.4 0.9 fusion.10
  41.3 0.9 convolution_bitcast_fusion.5
  42.2 0.9 convolution_bitcast_fusion.4
  43.0 0.9 convolution_bitcast_fusion.3
  43.9 5.2 %collective-permute-start.3 = (bf16[2,1,128,128]{3,2,1,0:T(8,128)(2,1)S(1)}, bf16[2,1,128,128]{3,2,1,0:T(8,128)(2,1)S(1)}, u32[]{:S(2)}, u32[]{:S(2)}) collective-permute-start(bf16[2,1,128,128]{3,2,1,0:T(8,128)(2,1)S(1)} %slice.447), channel_id=1, source_target_pairs={{0,1},{1,2},{2,3},{3,4},{4,5},{5,6},{6,7},{7,8},{8,9},{9,10},{10,1... | collective-permute-start | bytes 196616 | tf_op jit(solution)/shard_map/ppermute | solution.py:28
  49.2 1.4 copy.96
  50.6 1.9 concatenate.66
  53.9 3.2 collective-permute-start.4
  57.5 5.3 %collective-permute-done.4 = bf16[2,5,128,128]{3,2,1,0:T(8,128)(2,1)S(1)} collective-permute-done((bf16[2,5,128,128]{3,2,1,0:T(8,128)(2,1)S(1)}, bf16[2,5,128,128]{3,2,1,0:T(8,128)(2,1)S(1)}, u32[]{:S(2)}, u32[]{:S(2)}) %collective-permute-start.4) | collective-permute-done | bytes 327712 | tf_op jit(solution)/shard_map/ppermute | solution.py:28
  67.7 0.8 slice.406
  72.2 0.8 constant_dynamic-update-slice_fusion.17
  73.0 0.8 constant_dynamic-update-slice_fusion.16
  74.5 0.8 constant_dynamic-update-slice_fusion.14
  76.8 0.8 constant_dynamic-update-slice_fusion.11
  78.6 0.8 constant_dynamic-update-slice_fusion.8
  79.4 0.8 constant_dynamic-update-slice_fusion.7
  80.7 1.4 copy.95
  82.1 2.9 concatenate.67
  85.0 3.6 pad_maximum_fusion
  88.7 1.3 dynamic-slice
  90.0 1.3 dynamic-slice.2
  91.3 1.3 dynamic-slice.4
  92.7 0.8 convolution_multiply_fusion.5
  93.5 132.0 %all-reduce.12.cloned.1.call-done = f32[4,16,8,1728]{3,2,1,0:T(8,128)} async-done(((f32[4,16,8,1728]{3,2,1,0:T(8,128)}), f32[4,16,8,1728]{3,2,1,0:T(8,128)}) %all-reduce.12.cloned.1.call-update) | async-done | bytes 3538960
  225.5 1.6 constant_dynamic-slice_fusion.1
  227.1 0.8 copy.71
  227.9 0.9 fusion.6
  228.8 1.4 fusion.8
  230.2 112.4 %all-reduce.14.cloned.1.call-done = f32[4,1,8,1728]{3,0,1,2:T(4,128)} async-done(((f32[4,1,8,1728]{3,0,1,2:T(4,128)}), f32[4,1,8,1728]{3,0,1,2:T(4,128)}) %all-reduce.14.cloned.1.call-update) | async-done | bytes 221200
  342.6 1.4 constant_dynamic-slice_fusion
  344.0 35.2 %all-reduce.8 = bf16[4,1,1,1728]{3,2,1,0:T(2,128)(2,1)S(1)} all-reduce(f32[4,1,1,1728]{3,2,1,0:T(1,128)S(1)} %copy.72), channel_id=4, replica_groups=mesh['dp'=4,'tm'=8,'height'=16] {'dp'}, use_global_device_ids=true, to_apply=%region_5.6.clone | all-reduce | flops 6912 | bytes 41472
  379.9 48.0 %all_gather.6 = bf16[1,1,8,1728]{3,1,0,2:T(2,128)(2,1)S(1)} all-gather(bf16[1,1,1,1728]{3,1,0,2:T(2,128)(2,1)S(1)} %fusion.64), channel_id=1, replica_groups=mesh['dp'=4,'tm'=8,'height'=16] {'tm'}, dimensions={2}, use_global_device_ids=true | all-gather | bytes 31104 | tf_op jit(solution)/shard_map/all_gather | solution.py:171
  427.9 24.0 %all_gather.7 = bf16[1,16,8,1728]{3,2,0,1:T(8,128)(2,1)S(1)} all-gather(bf16[1,1,8,1728]{3,2,0,1:T(8,128)(2,1)S(1)} %copy.74), channel_id=1, replica_groups=mesh['dp'=4,'tm'=8,'height'=16] {'height'}, dimensions={1}, use_global_device_ids=true | all-gather | bytes 470016 | tf_op jit(solution)/shard_map/all_gather | solution.py:172
  451.9 1.0 reshape.211
  452.9 1.0 reshape.212
  (150 shorter events, 22.0 us)
Async XLA Ops:
  7.2 19.8 %copy-start = (bf16[1,2,4,128,128]{4,3,2,1,0:T(8,128)(2,1)S(1)}, bf16[1,2,4,128,128]{4,3,2,1,0:T(8,128)(2,1)}, u32[]{:S(2)}) copy-start(bf16[1,2,4,128,128]{4,3,2,1,0:T(8,128)(2,1)} %param.5) | copy-start | bytes 786436
  7.2 218.3 %all-reduce.12.cloned.1.call-start = ((), (), s32[]{:S(2)}) async-start(), calls=%async_computation | async-start | bytes 7340032
  8.1 18.8 %collective-permute-start = (bf16[2,1,128,128]{3,2,1,0:T(8,128)(2,1)S(1)}, bf16[2,1,128,128]{3,2,1,0:T(8,128)(2,1)S(1)}, u32[]{:S(2)}, u32[]{:S(2)}) collective-permute-start(bf16[2,1,128,128]{3,2,1,0:T(8,128)(2,1)S(1)} %get-tuple-element.17), channel_id=1, source_target_pairs={{0,1},{1,2},{2,3},{3,4},{4,5},{5,6},{6,7},{7,8},{8,9},{9,10},{10,1... | collective-permute-start | bytes 196616 | tf_op jit(solution)/shard_map/ppermute | solution.py:16
  11.6 15.3 %collective-permute-start.1 = (bf16[2,1,128,128]{3,2,1,0:T(8,128)(2,1)S(1)}, bf16[2,1,128,128]{3,2,1,0:T(8,128)(2,1)S(1)}, u32[]{:S(2)}, u32[]{:S(2)}) collective-permute-start(bf16[2,1,128,128]{3,2,1,0:T(8,128)(2,1)S(1)} %get-tuple-element.18), channel_id=1, source_target_pairs={{1,0},{2,1},{3,2},{4,3},{5,4},{6,5},{7,6},{8,7},{9,8},{10,9},{11,1... | collective-permute-start | bytes 196616 | tf_op jit(solution)/shard_map/ppermute | solution.py:18
  13.7 8.0 %collective-permute-start.5 = (bf16[1,1,64,128]{3,2,1,0:T(8,128)(2,1)S(1)}, bf16[1,1,64,128]{3,2,1,0:T(8,128)(2,1)S(1)}, u32[]{:S(2)}, u32[]{:S(2)}) collective-permute-start(bf16[1,1,64,128]{3,2,1,0:T(8,128)(2,1)S(1)} %slice.452), channel_id=1, source_target_pairs={{1,0},{2,1},{3,2},{4,3},{5,4},{6,5},{7,6},{8,7},{9,8},{10,9},{11,1... | collective-permute-start | bytes 49160 | tf_op jit(solution)/shard_map/ppermute | solution.py:28
  21.7 7.5 %collective-permute-start.6 = (bf16[1,3,64,128]{3,2,1,0:T(8,128)(2,1)S(1)}, bf16[1,3,64,128]{3,2,1,0:T(8,128)(2,1)S(1)}, u32[]{:S(2)}, u32[]{:S(2)}) collective-permute-start(bf16[1,3,64,128]{3,2,1,0:T(8,128)(2,1)S(1)} %pad_maximum_fusion.8), channel_id=1, source_target_pairs={{16,0},{32,16},{48,32},{64,48},{80,64},{96,80},{112,96},{17,1},{33... | collective-permute-start | bytes 147464 | tf_op jit(solution)/shard_map/ppermute | solution.py:28
  27.0 4.3 copy-start.1
  27.0 4.3 copy-start.4
  27.0 9.8 %collective-permute-start.2 = (bf16[2,6,128,128]{3,2,1,0:T(8,128)(2,1)S(1)}, bf16[2,6,128,128]{3,2,1,0:T(8,128)(2,1)S(1)}, u32[]{:S(2)}, u32[]{:S(2)}) collective-permute-start(bf16[2,6,128,128]{3,2,1,0:T(8,128)(2,1)S(1)} %pad_maximum_fusion.4), channel_id=1, source_target_pairs={{0,16},{16,32},{32,48},{48,64},{64,80},{80,96},{96,112},{1,17},{17... | collective-permute-start | bytes 1179656 | tf_op jit(solution)/shard_map/ppermute | solution.py:28
  43.9 8.6 %collective-permute-start.3 = (bf16[2,1,128,128]{3,2,1,0:T(8,128)(2,1)S(1)}, bf16[2,1,128,128]{3,2,1,0:T(8,128)(2,1)S(1)}, u32[]{:S(2)}, u32[]{:S(2)}) collective-permute-start(bf16[2,1,128,128]{3,2,1,0:T(8,128)(2,1)S(1)} %slice.447), channel_id=1, source_target_pairs={{0,1},{1,2},{2,3},{3,4},{4,5},{5,6},{6,7},{7,8},{8,9},{9,10},{10,1... | collective-permute-start | bytes 196616 | tf_op jit(solution)/shard_map/ppermute | solution.py:28
  50.6 6.6 %copy-start.3 = (bf16[1,1,2,64,128]{4,3,2,1,0:T(8,128)(2,1)S(1)}, bf16[1,1,2,64,128]{4,3,2,1,0:T(8,128)(2,1)}, u32[]{:S(2)}) copy-start(bf16[1,1,2,64,128]{4,3,2,1,0:T(8,128)(2,1)} %param.9) | copy-start | bytes 98308
  53.9 9.0 %collective-permute-start.4 = (bf16[2,5,128,128]{3,2,1,0:T(8,128)(2,1)S(1)}, bf16[2,5,128,128]{3,2,1,0:T(8,128)(2,1)S(1)}, u32[]{:S(2)}, u32[]{:S(2)}) collective-permute-start(bf16[2,5,128,128]{3,2,1,0:T(8,128)(2,1)S(1)} %pad_maximum_fusion.3), channel_id=1, source_target_pairs={{0,16},{16,32},{32,48},{48,64},{64,80},{80,96},{96,112},{1,17},{17... | collective-permute-start | bytes 983048 | tf_op jit(solution)/shard_map/ppermute | solution.py:28
  88.6 3.9 copy-start.2
  88.7 253.9 %all-reduce.14.cloned.1.call-start = ((), (), s32[]{:S(2)}) async-start(), calls=%async_computation.1 | async-start | bytes 458752
Sparse Core Ops, SparseCore 0:
  88.8 136.6 all-reduce.11
  228.4 114.1 all-reduce.13
where the time goes:
time: 462 us; the launch traced here: 461 us
  waiting for transfers between devices  253 us (55%)
  blocking collectives  107 us (23%)
  local copies, waits for them, and re-layouts  43.2 us (9%)
  starting transfers between devices  21.8 us (5%)
  between operations  16.9 us (4%)
  matrix products  10 us (2%)
  other arithmetic  8.16 us (2%)
    unnamed x4, waiting for transfers between devices  244 us
    all_gather x1, blocking collectives, body(): piece = lax.all_gather(piece, 'tm', axis=2, tiled=True)  48 us
    unnamed x1, blocking collectives  35.2 us
    all_gather x1, blocking collectives, body(): gathered = lax.all_gather(piece, 'height', axis=1, tiled=True).reshape(-1)  24 us
    unnamed x66, local copies, waits for them, and re-layouts  17 us
    ppermute x5, starting transfers between devices, shifted(): lax.ppermute(value, axis, [(source, source + steps) for source in range(l...  17 us
    slice x27, local copies, waits for them, and re-layouts, unfold(): padded[:, tap_row:tap_row + stride * (out_rows - 1) + 1:stride, tap_col:t...  9.5 us
  transfers between devices with their start and end apart: 9, of which 4 were waited for; matrix products, arithmetic and copies ran while one was open for 4% of the time, Pallas kernels for 0%

commit v1 on v0

--- a/solution.py
+++ b/solution.py
@@ -168,7 +168,9 @@
     piece = lax.psum_scatter(piece, "tm", scatter_dimension=2, tiled=True)
     piece = lax.psum_scatter(piece, "dp", scatter_dimension=0, tiled=True)
     piece = piece.astype(jnp.bfloat16)
-    piece = lax.all_gather(piece, "tm", axis=2, tiled=True)
+    piece = jnp.concatenate(
+        lax.all_to_all(jnp.stack([piece] * lax.axis_size("tm")), "tm", 0, 0), axis=2
+    )
     gathered = lax.all_gather(piece, "height", axis=1, tiled=True).reshape(-1)
     half = gathered.shape[0] // 2
     kernel_shape = (3, 3, 3, share, conv_first.shape[-1])

time: 462 us -> 438 us (0.948)
  the two profiles are of different devices: /device:TPU:32 before, /device:TPU:2 now
where the time goes in v1:
time: 438 us; the launch traced here: 437 us
  waiting for transfers between devices  266 us (61%)
  blocking collectives  55.9 us (13%)
  local copies, waits for them, and re-layouts  44.6 us (10%)
  starting transfers between devices  34.8 us (8%)
  between operations  16.9 us (4%)
  matrix products  10 us (2%)
  other arithmetic  8.96 us (2%)
    unnamed x4, waiting for transfers between devices  247 us
    unnamed x1, blocking collectives  32.2 us
    all_gather x1, blocking collectives, body(): gathered = lax.all_gather(piece, 'height', axis=1, tiled=True).reshape(-1)  23.7 us
    unnamed x68, local copies, waits for them, and re-layouts  17.8 us
    ppermute x5, starting transfers between devices, shifted(): lax.ppermute(value, axis, [(source, source + steps) for source in range(l...  16.4 us
    all_to_all x1, starting transfers between devices, body(): lax.all_to_all(jnp.stack([piece] * lax.axis_size('tm')), 'tm', 0, 0)  10.3 us
    slice x27, local copies, waits for them, and re-layouts, unfold(): padded[:, tap_row:tap_row + stride * (out_rows - 1) + 1:stride, tap_col:t...  9.51 us
    ppermute x5, waiting for transfers between devices, shifted(): lax.ppermute(value, axis, [(source, source + steps) for source in range(l...  9.2 us
  transfers between devices with their start and end apart: 10, of which 6 were waited for; matrix products, arithmetic and copies ran while one was open for 5% of the time, Pallas kernels for 0%

profile of v1, /device:TPU:2, one launch (start us, length us, event | category | flops | bytes accessed | tf_op | source)
XLA Modules:
  0.0 436.6 jit_solution(6358233052005914635)
XLA Ops:
  7.2 0.9 fusion.92
  8.1 3.5 collective-permute-start
  11.6 4.5 %collective-permute-start.1 = (bf16[2,1,128,128]{3,2,1,0:T(8,128)(2,1)S(1)}, bf16[2,1,128,128]{3,2,1,0:T(8,128)(2,1)S(1)}, u32[]{:S(2)}, u32[]{:S(2)}) collective-permute-start(bf16[2,1,128,128]{3,2,1,0:T(8,128)(2,1)S(1)} %get-tuple-element.18), channel_id=1, source_target_pairs={{1,0},{2,1},{3,2},{4,3},{5,4},{6,5},{7,6},{8,7},{9,8},{10,9},{11,1... | collective-permute-start | bytes 196616 | tf_op jit(solution)/shard_map/ppermute | solution.py:18
  16.1 0.8 fusion.60
  16.9 2.8 collective-permute-start.5
  19.7 0.8 reduce-window_clone.1
  21.5 1.2 fusion.89
  26.4 1.3 collective-permute-start.6
  27.8 4.7 %collective-permute-start.2 = (bf16[2,6,128,128]{3,2,1,0:T(8,128)(2,1)S(1)}, bf16[2,6,128,128]{3,2,1,0:T(8,128)(2,1)S(1)}, u32[]{:S(2)}, u32[]{:S(2)}) collective-permute-start(bf16[2,6,128,128]{3,2,1,0:T(8,128)(2,1)S(1)} %pad_maximum_fusion.4), channel_id=1, source_target_pairs={{0,16},{16,32},{32,48},{48,64},{64,80},{80,96},{96,112},{1,17},{17... | collective-permute-start | bytes 1179656 | tf_op jit(solution)/shard_map/ppermute | solution.py:28
  32.6 1.3 multiply_bitcast_fusion.1
  36.5 3.4 collective-permute-done.2
  40.9 0.8 convolution_multiply_fusion.1
  42.6 0.8 fusion.1
  43.4 0.9 fusion.10
  44.4 0.9 convolution_bitcast_fusion.5
  45.2 0.9 convolution_bitcast_fusion.4
  46.1 0.9 convolution_bitcast_fusion.3
  47.0 3.1 collective-permute-start.3
  50.2 1.4 copy.114
  51.6 1.9 concatenate.66
  53.4 1.8 collective-permute-done.3
  56.6 4.6 %collective-permute-start.4 = (bf16[2,5,128,128]{3,2,1,0:T(8,128)(2,1)S(1)}, bf16[2,5,128,128]{3,2,1,0:T(8,128)(2,1)S(1)}, u32[]{:S(2)}, u32[]{:S(2)}) collective-permute-start(bf16[2,5,128,128]{3,2,1,0:T(8,128)(2,1)S(1)} %pad_maximum_fusion.3), channel_id=1, source_target_pairs={{0,16},{16,32},{32,48},{48,64},{64,80},{80,96},{96,112},{1,17},{17... | collective-permute-start | bytes 983048 | tf_op jit(solution)/shard_map/ppermute | solution.py:28
  61.6 3.9 collective-permute-done.4
  70.4 0.8 slice.406
  75.7 0.8 constant_dynamic-update-slice_fusion.16
  78.0 0.8 constant_dynamic-update-slice_fusion.13
  78.8 0.8 constant_dynamic-update-slice_fusion.12
  81.3 0.8 constant_dynamic-update-slice_fusion.8
  83.4 1.4 copy.113
  84.8 2.9 concatenate.67
  87.7 3.6 pad_maximum_fusion
  91.4 1.3 dynamic-slice
  92.8 1.3 dynamic-slice.2
  94.0 1.3 dynamic-slice.4
  95.4 0.9 convolution_multiply_fusion.5
  96.3 129.1 %all-reduce.12.cloned.1.call-done = f32[4,16,8,1728]{3,2,1,0:T(8,128)} async-done(((f32[4,16,8,1728]{3,2,1,0:T(8,128)}), f32[4,16,8,1728]{3,2,1,0:T(8,128)}) %all-reduce.12.cloned.1.call-update) | async-done | bytes 3538960
  225.4 1.6 constant_dynamic-slice_fusion.1
  227.0 0.8 copy.90
  228.6 118.1 %all-reduce.14.cloned.1.call-done = f32[4,1,8,1728]{3,0,1,2:T(4,128)} async-done(((f32[4,1,8,1728]{3,0,1,2:T(4,128)}), f32[4,1,8,1728]{3,0,1,2:T(4,128)}) %all-reduce.14.cloned.1.call-update) | async-done | bytes 221200
  346.6 1.4 constant_dynamic-slice_fusion
  348.1 32.2 %all-reduce.8 = bf16[4,1,1,1728]{3,2,1,0:T(2,128)(2,1)S(1)} all-reduce(f32[4,1,1,1728]{3,2,1,0:T(1,128)S(1)} %copy.91), channel_id=5, replica_groups=mesh['dp'=4,'tm'=8,'height'=16] {'dp'}, use_global_device_ids=true, to_apply=%region_5.6.clone | all-reduce | flops 6912 | bytes 41472
  381.5 0.8 reduce.2
  383.1 10.3 %all-to-all-start = ((bf16[8,2,864]{2,1,0:T(2,128)(2,1)}), bf16[8,2,864]{2,1,0:T(2,128)(2,1)S(1)}, u32[]{:S(2)}, u32[]{:S(2)}) async-start(bf16[8,2,864]{2,1,0:T(2,128)(2,1)} %reshape.274), calls=%async_computation | async-start | bytes 57344 | tf_op jit(solution)/shard_map/all_to_all | solution.py:172
  393.4 1.5 fusion.8
  394.8 9.1 %all-to-all-done = bf16[8,2,864]{2,1,0:T(2,128)(2,1)S(1)} async-done(((bf16[8,2,864]{2,1,0:T(2,128)(2,1)}), bf16[8,2,864]{2,1,0:T(2,128)(2,1)S(1)}, u32[]{:S(2)}, u32[]{:S(2)}) %all-to-all-start) | async-done | bytes 27680 | tf_op jit(solution)/shard_map/all_to_all | solution.py:172
  404.1 23.7 %all-gather = bf16[128,1,1,1,1728]{4,0,3,2,1:T(8,128)(2,1)S(1)} all-gather(bf16[8,1,1,1,1728]{4,0,3,2,1:T(8,128)(2,1)S(1)} %copy.92), channel_id=2, replica_groups=mesh['dp'=4,'tm'=8,'height'=16] {'height'}, dimensions={0}, use_global_device_ids=true | all-gather | bytes 470016 | tf_op jit(solution)/shard_map/all_gather | solution.py:174
  427.8 1.0 reshape.218
  428.8 1.0 reshape.219
  (156 shorter events, 25.7 us)
Async XLA Ops:
  7.2 20.5 %copy-start = (bf16[1,2,4,128,128]{4,3,2,1,0:T(8,128)(2,1)S(1)}, bf16[1,2,4,128,128]{4,3,2,1,0:T(8,128)(2,1)}, u32[]{:S(2)}) copy-start(bf16[1,2,4,128,128]{4,3,2,1,0:T(8,128)(2,1)} %param.5) | copy-start | bytes 786436
  7.2 218.2 %all-reduce.12.cloned.1.call-start = ((), (), s32[]{:S(2)}) async-start(), calls=%async_computation.1 | async-start | bytes 7340032
  8.1 19.5 %collective-permute-start = (bf16[2,1,128,128]{3,2,1,0:T(8,128)(2,1)S(1)}, bf16[2,1,128,128]{3,2,1,0:T(8,128)(2,1)S(1)}, u32[]{:S(2)}, u32[]{:S(2)}) collective-permute-start(bf16[2,1,128,128]{3,2,1,0:T(8,128)(2,1)S(1)} %get-tuple-element.17), channel_id=1, source_target_pairs={{0,1},{1,2},{2,3},{3,4},{4,5},{5,6},{6,7},{7,8},{8,9},{9,10},{10,1... | collective-permute-start | bytes 196616 | tf_op jit(solution)/shard_map/ppermute | solution.py:16
  11.6 16.1 %collective-permute-start.1 = (bf16[2,1,128,128]{3,2,1,0:T(8,128)(2,1)S(1)}, bf16[2,1,128,128]{3,2,1,0:T(8,128)(2,1)S(1)}, u32[]{:S(2)}, u32[]{:S(2)}) collective-permute-start(bf16[2,1,128,128]{3,2,1,0:T(8,128)(2,1)S(1)} %get-tuple-element.18), channel_id=1, source_target_pairs={{1,0},{2,1},{3,2},{4,3},{5,4},{6,5},{7,6},{8,7},{9,8},{10,9},{11,1... | collective-permute-start | bytes 196616 | tf_op jit(solution)/shard_map/ppermute | solution.py:18
  16.9 9.5 %collective-permute-start.5 = (bf16[1,1,64,128]{3,2,1,0:T(8,128)(2,1)S(1)}, bf16[1,1,64,128]{3,2,1,0:T(8,128)(2,1)S(1)}, u32[]{:S(2)}, u32[]{:S(2)}) collective-permute-start(bf16[1,1,64,128]{3,2,1,0:T(8,128)(2,1)S(1)} %slice.452), channel_id=1, source_target_pairs={{1,0},{2,1},{3,2},{4,3},{5,4},{6,5},{7,6},{8,7},{9,8},{10,9},{11,1... | collective-permute-start | bytes 49160 | tf_op jit(solution)/shard_map/ppermute | solution.py:28
  26.4 6.2 %collective-permute-start.6 = (bf16[1,3,64,128]{3,2,1,0:T(8,128)(2,1)S(1)}, bf16[1,3,64,128]{3,2,1,0:T(8,128)(2,1)S(1)}, u32[]{:S(2)}, u32[]{:S(2)}) collective-permute-start(bf16[1,3,64,128]{3,2,1,0:T(8,128)(2,1)S(1)} %pad_maximum_fusion.8), channel_id=1, source_target_pairs={{16,0},{32,16},{48,32},{64,48},{80,64},{96,80},{112,96},{17,1},{33... | collective-permute-start | bytes 147464 | tf_op jit(solution)/shard_map/ppermute | solution.py:28
  27.8 6.9 %copy-start.1 = (bf16[3,3,3,128,128]{4,3,2,1,0:T(8,128)(2,1)S(1)}, bf16[3,3,3,128,128]{4,3,2,1,0:T(8,128)(2,1)}, u32[]{:S(2)}) copy-start(bf16[3,3,3,128,128]{4,3,2,1,0:T(8,128)(2,1)} %param.8) | copy-start | bytes 2654212
  27.8 6.9 %copy-start.4 = (pred[8,18]{0,1:T(8,128)(4,1)S(1)}, pred[8,18]{0,1:T(8,128)(4,1)}, u32[]{:S(2)}) copy-start(pred[8,18]{0,1:T(8,128)(4,1)} %constant.53) | copy-start | bytes 436
  27.8 12.1 %collective-permute-start.2 = (bf16[2,6,128,128]{3,2,1,0:T(8,128)(2,1)S(1)}, bf16[2,6,128,128]{3,2,1,0:T(8,128)(2,1)S(1)}, u32[]{:S(2)}, u32[]{:S(2)}) collective-permute-start(bf16[2,6,128,128]{3,2,1,0:T(8,128)(2,1)S(1)} %pad_maximum_fusion.4), channel_id=1, source_target_pairs={{0,16},{16,32},{32,48},{48,64},{64,80},{80,96},{96,112},{1,17},{17... | collective-permute-start | bytes 1179656 | tf_op jit(solution)/shard_map/ppermute | solution.py:28
  47.0 8.3 %collective-permute-start.3 = (bf16[2,1,128,128]{3,2,1,0:T(8,128)(2,1)S(1)}, bf16[2,1,128,128]{3,2,1,0:T(8,128)(2,1)S(1)}, u32[]{:S(2)}, u32[]{:S(2)}) collective-permute-start(bf16[2,1,128,128]{3,2,1,0:T(8,128)(2,1)S(1)} %slice.447), channel_id=1, source_target_pairs={{0,1},{1,2},{2,3},{3,4},{4,5},{5,6},{6,7},{7,8},{8,9},{9,10},{10,1... | collective-permute-start | bytes 196616 | tf_op jit(solution)/shard_map/ppermute | solution.py:28
  51.5 9.8 %copy-start.3 = (bf16[1,1,2,64,128]{4,3,2,1,0:T(8,128)(2,1)S(1)}, bf16[1,1,2,64,128]{4,3,2,1,0:T(8,128)(2,1)}, u32[]{:S(2)}) copy-start(bf16[1,1,2,64,128]{4,3,2,1,0:T(8,128)(2,1)} %param.9) | copy-start | bytes 98308
  56.6 9.0 %collective-permute-start.4 = (bf16[2,5,128,128]{3,2,1,0:T(8,128)(2,1)S(1)}, bf16[2,5,128,128]{3,2,1,0:T(8,128)(2,1)S(1)}, u32[]{:S(2)}, u32[]{:S(2)}) collective-permute-start(bf16[2,5,128,128]{3,2,1,0:T(8,128)(2,1)S(1)} %pad_maximum_fusion.3), channel_id=1, source_target_pairs={{0,16},{16,32},{32,48},{48,64},{64,80},{80,96},{96,112},{1,17},{17... | collective-permute-start | bytes 983048 | tf_op jit(solution)/shard_map/ppermute | solution.py:28
  91.3 3.9 copy-start.2
  91.4 255.3 %all-reduce.14.cloned.1.call-start = ((), (), s32[]{:S(2)}) async-start(), calls=%async_computation.2 | async-start | bytes 458752
  383.1 20.9 %all-to-all-start = ((bf16[8,2,864]{2,1,0:T(2,128)(2,1)}), bf16[8,2,864]{2,1,0:T(2,128)(2,1)S(1)}, u32[]{:S(2)}, u32[]{:S(2)}) async-start(bf16[8,2,864]{2,1,0:T(2,128)(2,1)} %reshape.274), calls=%async_computation | async-start | bytes 57344 | tf_op jit(solution)/shard_map/all_to_all | solution.py:172
Sparse Core Ops, SparseCore 0:
  91.5 133.8 all-reduce.11
  228.3 118.2 all-reduce.13
